TPU v7x, 512 devices: a whole 4x8x8 slice. The times are simulated.
512 devices in a mesh: grp: 16 (over z, core), dev: 32 (over x, y).
Axes of the slice: x: 4, y: 8, z: 8, core: 2. Of those that a mesh axis runs over, the one named last changes fastest.
Arguments:
- ssm_input: bfloat16 [4096, 4096], P('grp', 'dev'), may hold values from -6 to 6
- gate_input: bfloat16 [4096, 4096], P('grp', 'dev'), may hold values from -6 to 6
- step_size: float32 [4096, 64], P('grp', 'dev'), may hold values from 6.1035156e-05 to 0.3375
- decay_rate: float32 [64], P('dev'), may hold values from 0.5 to 2
- in_coeff: bfloat16 [4096, 128], P('grp'), may hold values from -6 to 6
- out_coeff: bfloat16 [4096, 128], P('grp'), may hold values from -6 to 6
- skip_gain: float32 [64], P('dev'), may hold values from 0.5 to 3
- norm_gain: float32 [4096], P('dev'), may hold values from 0.5 to 1.5
- out_proj: bfloat16 [4096, 2048], P(None, 'dev'), may hold values from -0.09375 to 0.09375
- residual: bfloat16 [4096, 2048], P(('grp', 'dev')), may hold values from -6 to 6
- ffn_gain: float32 [2048], replicated, may hold values from 0.5 to 1.5
- router: float32 [2048, 16], replicated, may hold values from -0.125 to 0.125
- routes: int32 [4096, 2], P(('grp', 'dev')), may hold values from 0 to 15, all different within a row; in each aligned block of 8 rows (0 to 7, 8 to 15, ...) at most 2 rows name the same one
- gate_weight: bfloat16 [16, 2048, 8192], P('grp', None, 'dev'), may hold values from -0.125 to 0.125
- up_weight: bfloat16 [16, 2048, 8192], P('grp', None, 'dev'), may hold values from -0.125 to 0.125
- down_weight: bfloat16 [16, 8192, 2048], P('grp', 'dev'), may hold values from -0.0625 to 0.0625
Outputs:
- moe_out: bfloat16 [4096, 2048], P(('grp', 'dev'))
Inputs may be any that keep to these rules, and one draw needn't show every extreme that they name: `routes`: each row names two different experts; among the 8 rows of one dispatch block of consecutive tokens no expert is named more than 2 times, a bound that some block reaches.
All inputs are finite; a program needn't handle non-finite values.
Results may differ from a plain program's by a relative error of at most 0.012.
Values may be sent and summed in bfloat16 or wider, within the bound.
No kernel may reach another device: no remote copies, remote signals or barrier semaphores. Data moves between devices by JAX's collectives and lax.ppermute only.
A program may use at most 64 MiB of HBM per device.

v0:
```python
import jax
import jax.numpy as jnp
from jax import lax
from jax.sharding import Mesh
from jax.sharding import PartitionSpec as P

DEV = ("dev_0", "dev_1")
GRP_DEV = ("grp", "dev_0", "dev_1")
EPSILON = 1e-05
HIGHEST_PREC = lax.Precision.HIGHEST


def side_by_side(arrays, axis, dim, along):
    columns = [a.reshape(*a.shape[:along], -1) for a in arrays]
    both = jnp.concatenate(columns, axis=along)
    filled, at, finished = (lax.all_gather(both, axis, axis=dim, tiled=True), 0, [])
    for a, column in zip(arrays, columns):
        piece = filled[..., at : at + column.shape[along]]
        finished.append(piece.reshape(*piece.shape[:along], *a.shape[along:]))
        at += column.shape[along]
    return tuple(finished)


def sent_to_all(shard, axis):
    peers = lax.axis_size(axis)
    return lax.all_to_all(
        jnp.broadcast_to(shard[None], (peers, *shard.shape)), axis, 0, 0, tiled=True
    )


def of_everyone(shard, axis):
    everything = sent_to_all(shard, axis)
    return jnp.sum(everything, axis=0)


def in_order(tiles, dim):
    dims = list(tiles.shape[1:])
    dims[dim] *= tiles.shape[0]
    return jnp.moveaxis(tiles, 0, dim).reshape(dims)


def collect(shard, axis, dim):
    return in_order(sent_to_all(shard, axis), dim)


def sum_by_axis(terms, axes):
    total = terms.astype(jnp.bfloat16)
    for axis in axes:
        total = lax.psum_scatter(total, axis, scatter_dimension=0, tiled=True)
    return total.astype(jnp.float32)


def ring_gather(shard, axis):
    size = lax.axis_size(axis)
    forward, backward, pieces = (shard, shard, {0: shard})
    for step in range(1, size // 2 + 1):
        forward = lax.ppermute(forward, axis, [(i, (i + 1) % size) for i in range(size)])
        pieces[-step] = forward
        if step < size - step:
            backward = lax.ppermute(backward, axis, [(i, (i - 1) % size) for i in range(size)])
            pieces[step] = backward
    offsets = list(range(-(size // 2), size - size // 2))
    stacked = jnp.stack([pieces[o] for o in offsets])
    doubled = jnp.concatenate([stacked, stacked])
    start = (-offsets[0] - lax.axis_index(axis)) % size
    return lax.dynamic_slice_in_dim(doubled, start, size, 0)


def rms_scale(values, gain_vec):
    return (
        values * lax.rsqrt(jnp.mean(values * values, axis=-1, keepdims=True) + EPSILON) * gain_vec
    )


def slot_tables(routes_block, expert_count, slot_cap):
    blocks, row_total = (routes_block.shape[0], routes_block.shape[1])
    flat_routes = routes_block.reshape(blocks, row_total * 2)
    onehot = (
        flat_routes[:, :, None] == jnp.arange(expert_count, dtype=jnp.int32)[None, None, :]
    ).astype(jnp.int32)
    earlier = jnp.cumsum(onehot, axis=1) - onehot
    slot_rank = jnp.sum(earlier * onehot, axis=2)
    slot_index = (flat_routes * slot_cap + slot_rank).reshape(blocks, row_total, 2)
    placed = (
        slot_index[:, :, :, None]
        == jnp.arange(expert_count * slot_cap, dtype=jnp.int32)[None, None, None, :]
    )
    return placed.astype(jnp.float32)


def shards(
    ssm_input,
    gate_input,
    step_size,
    decay_rate,
    in_coeff,
    out_coeff,
    skip_gain,
    norm_gain,
    out_proj,
    residual,
    ffn_gain,
    router,
    routes,
    gate_weight,
    up_weight,
    down_weight,
):
    tok_rows = ssm_input.shape[0]
    head_count = step_size.shape[1]
    head_width = ssm_input.shape[1] // head_count
    dev_count = lax.axis_size(DEV)
    inner_dim = ssm_input.shape[1] * dev_count
    block_rows = residual.shape[0]
    model_dim = residual.shape[1]
    experts = lax.axis_size("grp")
    slot_cap = max(2, 4 * block_rows // experts)
    group_slots = experts * slot_cap
    inputs_f = ssm_input.astype(jnp.float32).reshape(tok_rows, head_count, head_width)
    in_float = in_coeff.astype(jnp.float32)
    out_float = out_coeff.astype(jnp.float32)
    log_rate = -(step_size * decay_rate[None, :])
    cumulative = jnp.cumsum(log_rate, axis=0)
    causal = (jnp.arange(tok_rows)[:, None] >= jnp.arange(tok_rows)[None, :])[:, :, None]
    spread = cumulative[:, None, :] - cumulative[None, :, :]
    decay_pair = jnp.where(causal, jnp.exp(jnp.where(causal, spread, 0.0)), 0.0)
    scores = jnp.dot(out_coeff, in_coeff.T, preferred_element_type=jnp.float32)
    mixing = decay_pair * scores[:, :, None] * step_size[None, :, :]
    inside = jnp.einsum("tuh,uhp->thp", mixing, inputs_f, precision=HIGHEST_PREC)
    to_end = jnp.exp(cumulative[-1][None, :] - cumulative) * step_size
    own_state = jnp.einsum("uh,uhp,un->hpn", to_end, inputs_f, in_float, precision=HIGHEST_PREC)
    own_log = cumulative[-1]
    group_logs, group_states = tuple(
        (
            part.astype(jnp.float32)
            for part in side_by_side(
                (own_log[None].astype(jnp.bfloat16), own_state[None].astype(jnp.bfloat16)),
                "grp",
                0,
                2,
            )
        )
    )
    group_index = jnp.arange(group_logs.shape[0])
    my_group = lax.axis_index("grp")
    inclusive = jnp.cumsum(group_logs, axis=0)
    exclusive = inclusive - group_logs
    before_me = jnp.sum(jnp.where((group_index == my_group)[:, None], exclusive, 0.0), axis=0)
    earlier_mask = (group_index < my_group)[:, None]
    weighting = jnp.where(
        earlier_mask, jnp.exp(jnp.where(earlier_mask, before_me[None, :] - inclusive, 0.0)), 0.0
    )
    entering = jnp.einsum("gh,ghpn->hpn", weighting, group_states, precision=HIGHEST_PREC)
    carried = jnp.exp(cumulative)[:, :, None] * jnp.einsum(
        "hpn,tn->thp", entering, out_float, precision=HIGHEST_PREC
    )
    ssm_out = inside + carried + skip_gain[None, :, None] * inputs_f
    gated_out = ssm_out.reshape(tok_rows, head_count * head_width) * jax.nn.silu(
        gate_input.astype(jnp.float32)
    )
    gated_gain = gated_out * norm_gain[None, :]
    squares = gated_out * gated_out
    proj_rows = lax.all_to_all(
        out_proj.reshape(dev_count, -1, out_proj.shape[1]), DEV, 0, 0, tiled=True
    )
    chan = proj_rows.shape[1]
    proj_rows = jnp.transpose(proj_rows, (1, 0, 2)).reshape(chan, model_dim)
    lane_pad = 128
    square_cols = (jnp.arange(lane_pad) == 0).astype(jnp.bfloat16)
    rhs = jnp.concatenate(
        [
            jnp.concatenate([proj_rows, jnp.zeros((chan, lane_pad), jnp.bfloat16)], axis=1),
            jnp.concatenate(
                [
                    jnp.zeros((chan, model_dim), jnp.bfloat16),
                    jnp.broadcast_to(square_cols, (chan, lane_pad)),
                ],
                axis=1,
            ),
        ],
        axis=0,
    )
    lhs = jnp.concatenate([gated_gain, squares], axis=1).astype(jnp.bfloat16)
    payload = jnp.dot(lhs, rhs, preferred_element_type=jnp.float32).astype(jnp.bfloat16)
    x_count = lax.axis_size("dev_0")
    y_count = lax.axis_size("dev_1")
    by_x = lax.all_to_all(
        payload.reshape(x_count, y_count, block_rows, payload.shape[1]), "dev_0", 0, 0, tiled=True
    )
    both_weight = jnp.concatenate([gate_weight[0], up_weight[0]], axis=1)
    by_x, both_weight = lax.optimization_barrier((by_x, both_weight))
    by_x = jnp.sum(by_x.astype(jnp.float32), axis=0).astype(jnp.bfloat16)
    landed = lax.all_to_all(by_x, "dev_1", 0, 0, tiled=True)
    landed = jnp.sum(landed.astype(jnp.float32), axis=0)
    summed_proj = landed[:, :model_dim]
    token_squares = landed[:, model_dim]
    mamba_out = (summed_proj * lax.rsqrt(token_squares / inner_dim + EPSILON)[:, None]).astype(
        jnp.bfloat16
    )
    hidden_res = (residual.astype(jnp.float32) + mamba_out.astype(jnp.float32)).astype(jnp.bfloat16)
    hidden_float = hidden_res.astype(jnp.float32)
    normed = rms_scale(hidden_float, ffn_gain).astype(jnp.bfloat16)
    logits = jnp.dot(normed.astype(jnp.float32), router, precision=HIGHEST_PREC)
    expert_ids = jnp.arange(experts, dtype=jnp.int32)[None, :]
    first_logit = jnp.sum(logits * (routes[:, 0:1] == expert_ids).astype(jnp.float32), axis=1)
    second_logit = jnp.sum(logits * (routes[:, 1:2] == expert_ids).astype(jnp.float32), axis=1)
    first_prob = jax.nn.sigmoid(first_logit - second_logit)
    second_prob = 1.0 - first_prob
    placed = slot_tables(routes[None], experts, slot_cap)[0]
    filled = jnp.sum(placed, axis=1)
    outgoing = jnp.dot(
        filled.T.astype(jnp.bfloat16), normed, preferred_element_type=jnp.float32
    ).astype(jnp.bfloat16)
    outgoing = outgoing.reshape(experts, slot_cap, model_dim)
    outgoing = jnp.broadcast_to(outgoing[:, None], (experts, x_count, slot_cap, model_dim))
    arrived = lax.all_to_all(
        outgoing.reshape(experts * x_count, slot_cap, model_dim), ("grp", "dev_0"), 0, 0, tiled=True
    )
    all_rows = lax.all_gather(arrived.reshape(-1, model_dim), "dev_1", axis=0, tiled=True)
    hid_units = gate_weight.shape[2]
    both_act = jnp.dot(all_rows, both_weight, preferred_element_type=jnp.float32)
    hidden = (jax.nn.silu(both_act[:, :hid_units]) * both_act[:, hid_units:]).astype(jnp.bfloat16)
    hidden = lax.optimization_barrier(hidden)
    partial_down = jnp.dot(hidden, down_weight[0], preferred_element_type=jnp.float32)
    summed = lax.psum_scatter(
        partial_down.astype(jnp.bfloat16), "dev_1", scatter_dimension=0, tiled=True
    )
    landed_back = lax.all_to_all(
        summed.reshape(experts * x_count, slot_cap, model_dim), ("grp", "dev_0"), 0, 0, tiled=True
    )
    returned = jnp.sum(
        landed_back.reshape(experts, x_count, slot_cap, model_dim).astype(jnp.float32), axis=1
    )
    weights = first_prob[:, None] * placed[:, 0, :] + second_prob[:, None] * placed[:, 1, :]
    contrib = jnp.dot(weights, returned.reshape(group_slots, model_dim), precision=HIGHEST_PREC)
    return (hidden_float + contrib).astype(jnp.bfloat16)


def solution(mesh):
    torus = Mesh(mesh.devices.reshape(mesh.shape["grp"], 4, 8), ("grp", "dev_0", "dev_1"))
    in_specs = (
        P("grp", DEV),
        P("grp", DEV),
        P("grp", DEV),
        P(DEV),
        P("grp", None),
        P("grp", None),
        P(DEV),
        P(DEV),
        P(None, DEV),
        P(GRP_DEV, None),
        P(),
        P(),
        P(GRP_DEV, None),
        P("grp", None, DEV),
        P("grp", None, DEV),
        P("grp", DEV, None),
    )
    out_specs = P(GRP_DEV, None)
    return jax.shard_map(
        shards, mesh=torus, in_specs=in_specs, out_specs=out_specs, check_vma=False
    )
```

profile of v0, /device:TPU:1, one launch (start us, length us, event | category | flops | bytes accessed | tf_op | source)
XLA Modules:
  0.0 269.2 jit_solution(579986233755267181)
XLA Ops:
  6.5 2.1 copy_bitcast_fusion
  8.6 10.5 %all-to-all-start = ((bf16[32,128,64]{1,2,0:T(8,128)(2,1)}), bf16[32,128,64]{1,2,0:T(8,128)(2,1)S(1)}, u32[]{:S(2)}, u32[]{:S(2)}) async-start(bf16[32,128,64]{1,2,0:T(8,128)(2,1)} %copy_bitcast_fusion), calls=%async_computation | async-start | bytes 1048576 | tf_op jit(solution)/shard_map/all_to_all | solution.py:163
  19.3 0.6 reduce-window.6
  21.1 25.4 %all_gather.6 = bf16[16,2,8193]{2,1,0:T(2,128)(2,1)S(1)} all-gather(bf16[1,2,8193]{2,1,0:T(2,128)(2,1)S(1)} %pad_maximum_fusion.1), channel_id=1, replica_groups=mesh['grp'=16,'dev_0'=4,'dev_1'=8] {'grp'}, dimensions={0}, use_global_device_ids=true | all-gather | bytes 557124 | tf_op jit(solution)/shard_map/all_gather | solution.py:16
  46.5 0.7 slice.56
  47.7 0.4 reshape.235
  48.1 0.6 fusion.13
  48.7 0.2 fusion.4
  49.2 0.6 fusion.3
  50.0 0.3 concatenate.28
  50.3 1.5 convolution_convert_fusion
  51.9 4.4 %all-to-all-start.1 = ((bf16[4,8,8,2176]{3,2,1,0:T(8,128)(2,1)}), bf16[4,8,8,2176]{3,2,1,0:T(8,128)(2,1)S(1)}, u32[]{:S(2)}, u32[]{:S(2)}) async-start(bf16[4,8,8,2176]{3,2,1,0:T(8,128)(2,1)} %bitcast.16), calls=%async_computation.1 | async-start | bytes 2228224 | tf_op jit(solution)/shard_map/all_to_all | solution.py:187
  56.5 2.7 %pad_maximum_fusion = bf16[2048,512]{1,0:T(8,128)(2,1)} fusion(bf16[2048,256]{1,0:T(8,128)(2,1)S(1)} %bitcast.83, bf16[2048,256]{1,0:T(8,128)(2,1)} %bitcast.84), kind=kLoop, calls=%fused_computation.7 | loop fusion | flops 4194304 | bytes 4194304 | tf_op jit(solution)/shard_map/concatenate | solution.py:190
  59.2 12.6 %all-to-all-done.1 = bf16[4,8,8,2176]{3,2,1,0:T(8,128)(2,1)S(1)} async-done(((bf16[4,8,8,2176]{3,2,1,0:T(8,128)(2,1)}), bf16[4,8,8,2176]{3,2,1,0:T(8,128)(2,1)S(1)}, u32[]{:S(2)}, u32[]{:S(2)}) %all-to-all-start.1) | async-done | bytes 1114144 | tf_op jit(solution)/shard_map/all_to_all | solution.py:187
  71.8 0.9 reduce_sum.87
  72.7 6.4 %all-to-all-start.2 = ((bf16[8,8,2176]{2,1,0:T(8,128)(2,1)}), bf16[8,8,2176]{2,1,0:T(8,128)(2,1)S(1)}, u32[]{:S(2)}, u32[]{:S(2)}) async-start(bf16[8,8,2176]{2,1,0:T(8,128)(2,1)} %reduce_sum.87), calls=%async_computation.2 | async-start | bytes 557056 | tf_op jit(solution)/shard_map/all_to_all | solution.py:193
  79.6 9.8 %all-to-all-done.2 = bf16[8,8,2176]{2,1,0:T(8,128)(2,1)S(1)} async-done(((bf16[8,8,2176]{2,1,0:T(8,128)(2,1)}), bf16[8,8,2176]{2,1,0:T(8,128)(2,1)S(1)}, u32[]{:S(2)}, u32[]{:S(2)}) %all-to-all-start.2) | async-done | bytes 278560 | tf_op jit(solution)/shard_map/all_to_all | solution.py:193
  89.8 0.2 convolution_convert_fusion.2
  90.2 0.3 broadcast_in_dim.79
  90.5 24.0 %all_to_all.25 = bf16[64,2,2048]{2,1,0:T(2,128)(2,1)} all-to-all(bf16[64,2,2048]{2,1,0:T(2,128)(2,1)S(1)} %bitcast.82), channel_id=1, replica_groups=mesh['grp'=16,'dev_0'=4,'dev_1'=8] {'grp','dev_0'}, dimensions={0} | all-to-all | bytes 1048576 | tf_op jit(solution)/shard_map/all_to_all | solution.py:216
  114.5 2.0 reshape.241
  116.6 48.8 %all-gather.2.cloned.1.call-done = bf16[1024,2048]{1,0:T(8,128)(2,1)} async-done(((bf16[128,2048]{1,0:T(8,128)(2,1)}), bf16[1024,2048]{1,0:T(8,128)(2,1)}) %all-gather.2.cloned.1.call-update) | async-done | bytes 4194320 | tf_op jit(solution)/shard_map/all_gather | solution.py:219
  165.4 4.5 %fusion.63 = f32[1024,512]{1,0:T(8,128)S(1)} fusion(bf16[1024,2048]{1,0:T(8,128)(2,1)} %all-gather.2.cloned.1.call-done, bf16[2048,512]{1,0:T(8,128)(2,1)S(1)} %copy-done.1), kind=kOutput, calls=%fused_computation.114 | convolution fusion | flops 2147483648 | bytes 8388608 | tf_op jit(solution)/shard_map/dot_general | solution.py:221
  169.9 0.3 fusion.10
  170.3 3.2 %convolution_convert_fusion.1 = bf16[1024,2048]{1,0:T(8,128)(2,1)} fusion(bf16[1024,256]{1,0:T(8,128)(2,1)S(1)} %fusion.10, bf16[1,256,2048]{2,1,0:T(8,128)(2,1)S(1)} %copy-done), kind=kOutput, calls=%fused_computation.1 | convolution fusion | flops 1075838976 | bytes 5767168 | tf_op jit(solution)/shard_map/dot_general | solution.py:224
  173.5 56.8 %reduce-scatter.2.cloned.1.call-done = bf16[128,2048]{1,0:T(8,128)(2,1)} async-done(((bf16[1024,2048]{1,0:T(8,128)(2,1)}), bf16[128,2048]{1,0:T(8,128)(2,1)}) %reduce-scatter.2.cloned.1.call-update) | async-done | bytes 524304 | tf_op jit(solution)/shard_map/reduce_scatter | solution.py:225
  230.3 2.2 reshape.242
  232.5 11.0 %all-to-all-start.4 = ((bf16[64,2,2048]{2,1,0:T(2,128)(2,1)}), bf16[64,2,2048]{2,1,0:T(2,128)(2,1)S(1)}, u32[]{:S(2)}, u32[]{:S(2)}) async-start(bf16[64,2,2048]{2,1,0:T(2,128)(2,1)} %reshape.242), calls=%async_computation.5 | async-start | bytes 1048576 | tf_op jit(solution)/shard_map/all_to_all | solution.py:228
  243.6 0.3 select_reduce_fusion.2
  244.0 16.8 %all-to-all-done.4 = bf16[64,2,2048]{2,1,0:T(2,128)(2,1)S(1)} async-done(((bf16[64,2,2048]{2,1,0:T(2,128)(2,1)}), bf16[64,2,2048]{2,1,0:T(2,128)(2,1)S(1)}, u32[]{:S(2)}, u32[]{:S(2)}) %all-to-all-start.4) | async-done | bytes 524320 | tf_op jit(solution)/shard_map/all_to_all | solution.py:228
  260.8 0.5 convert_reduce_fusion
  261.4 0.9 fusion.1
  (81 shorter events, 3.8 us)
Async XLA Ops:
  6.5 163.7 %copy-start = (bf16[1,256,2048]{2,1,0:T(8,128)(2,1)S(1)}, bf16[1,256,2048]{2,1,0:T(8,128)(2,1)}, u32[]{:S(2)}) copy-start(bf16[1,256,2048]{2,1,0:T(8,128)(2,1)} %param.31) | copy-start | bytes 3145732
  6.5 12.6 %copy-start.9 = (f32[256,2]{0,1:T(2,128)S(1)}, f32[256,2]{0,1:T(2,128)}, u32[]{:S(2)}) copy-start(f32[256,2]{0,1:T(2,128)} %param.18) | copy-start | bytes 6148
  6.5 12.6 %copy-start.12 = (f32[2]{0:T(128)S(1)}, f32[2]{0:T(128)}, u32[]{:S(2)}) copy-start(f32[2]{0:T(128)} %param.19) | copy-start | bytes 28
  6.5 14.0 %copy-start.6 = (bf16[256,128]{1,0:T(8,128)(2,1)S(1)}, bf16[256,128]{1,0:T(8,128)(2,1)}, u32[]{:S(2)}) copy-start(bf16[256,128]{1,0:T(8,128)(2,1)} %param.16) | copy-start | bytes 196612
  6.5 14.2 %copy-start.3 = (bf16[256,128]{1,0:T(8,128)(2,1)S(1)}, bf16[256,128]{1,0:T(8,128)(2,1)}, u32[]{:S(2)}) copy-start(bf16[256,128]{1,0:T(8,128)(2,1)} %param.20) | copy-start | bytes 196612
  8.6 41.4 %all-to-all-start = ((bf16[32,128,64]{1,2,0:T(8,128)(2,1)}), bf16[32,128,64]{1,2,0:T(8,128)(2,1)S(1)}, u32[]{:S(2)}, u32[]{:S(2)}) async-start(bf16[32,128,64]{1,2,0:T(8,128)(2,1)} %copy_bitcast_fusion), calls=%async_computation | async-start | bytes 1048576 | tf_op jit(solution)/shard_map/all_to_all | solution.py:163
  19.1 29.5 %copy-start.4 = (bf16[256,128]{1,0:T(8,128)(2,1)S(1)}, bf16[256,128]{1,0:T(8,128)(2,1)}, u32[]{:S(2)}) copy-start(bf16[256,128]{1,0:T(8,128)(2,1)} %param.21) | copy-start | bytes 196612
  20.9 28.2 %copy-start.14 = (f32[2]{0:T(128)S(1)}, f32[2]{0:T(128)}, u32[]{:S(2)}) copy-start(f32[2]{0:T(128)} %param.22) | copy-start | bytes 28
  47.2 2.7 %copy-start.5 = (bf16[256,128]{1,0:T(8,128)(2,1)S(1)}, bf16[256,128]{1,0:T(8,128)(2,1)}, u32[]{:S(2)}) copy-start(bf16[256,128]{1,0:T(8,128)(2,1)} %param.17) | copy-start | bytes 196612
  47.2 2.7 copy-start.11
  51.9 4.4 %copy-start.10 = (s32[8,2]{0,1:T(2,128)S(1)}, s32[8,2]{0,1:T(2,128)}, u32[]{:S(2)}) copy-start(s32[8,2]{0,1:T(2,128)} %param.28) | copy-start | bytes 196
  51.9 4.6 %copy-start.2 = (bf16[1,2048,256]{2,1,0:T(8,128)(2,1)S(1)}, bf16[1,2048,256]{2,1,0:T(8,128)(2,1)}, u32[]{:S(2)}) copy-start(bf16[1,2048,256]{2,1,0:T(8,128)(2,1)} %param.30) | copy-start | bytes 3145732
  51.9 19.9 %all-to-all-start.1 = ((bf16[4,8,8,2176]{3,2,1,0:T(8,128)(2,1)}), bf16[4,8,8,2176]{3,2,1,0:T(8,128)(2,1)S(1)}, u32[]{:S(2)}, u32[]{:S(2)}) async-start(bf16[4,8,8,2176]{3,2,1,0:T(8,128)(2,1)} %bitcast.16), calls=%async_computation.1 | async-start | bytes 2228224 | tf_op jit(solution)/shard_map/all_to_all | solution.py:187
  59.2 30.4 %copy-start.7 = (bf16[8,2048]{1,0:T(8,128)(2,1)S(1)}, bf16[8,2048]{1,0:T(8,128)(2,1)}, u32[]{:S(2)}) copy-start(bf16[8,2048]{1,0:T(8,128)(2,1)} %param.25) | copy-start | bytes 98308
  59.2 30.6 %copy-start.8 = (f32[2048]{0:T(1024)S(1)}, f32[2048]{0:T(1024)}, u32[]{:S(2)}) copy-start(f32[2048]{0:T(1024)} %param.26) | copy-start | bytes 24580
  72.7 16.8 %all-to-all-start.2 = ((bf16[8,8,2176]{2,1,0:T(8,128)(2,1)}), bf16[8,8,2176]{2,1,0:T(8,128)(2,1)S(1)}, u32[]{:S(2)}, u32[]{:S(2)}) async-start(bf16[8,8,2176]{2,1,0:T(8,128)(2,1)} %reduce_sum.87), calls=%async_computation.2 | async-start | bytes 557056 | tf_op jit(solution)/shard_map/all_to_all | solution.py:193
  79.0 86.4 %all-gather.2.cloned.1.call-start = ((), (), s32[]{:S(2)}) async-start(), calls=%async_computation.6 | async-start | bytes 4718592 | tf_op jit(solution)/shard_map/all_gather | solution.py:219
  79.6 85.8 %copy-start.1 = (bf16[2048,512]{1,0:T(8,128)(2,1)S(1)}, bf16[2048,512]{1,0:T(8,128)(2,1)}, u32[]{:S(2)}) copy-start(bf16[2048,512]{1,0:T(8,128)(2,1)} %pad_maximum_fusion) | copy-start | bytes 6291460
  116.6 113.8 %reduce-scatter.2.cloned.1.call-start = ((), (), s32[]{:S(2)}) async-start(), calls=%async_computation.7 | async-start | bytes 4718592 | tf_op jit(solution)/shard_map/reduce_scatter | solution.py:225
  173.5 70.1 %copy-start.13 = (f32[2048,16]{0,1:T(8,128)S(1)}, f32[2048,16]{0,1:T(8,128)}, u32[]{:S(2)}) copy-start(f32[2048,16]{0,1:T(8,128)} %param.27) | copy-start | bytes 393220
  232.5 28.2 %all-to-all-start.4 = ((bf16[64,2,2048]{2,1,0:T(2,128)(2,1)}), bf16[64,2,2048]{2,1,0:T(2,128)(2,1)S(1)}, u32[]{:S(2)}, u32[]{:S(2)}) async-start(bf16[64,2,2048]{2,1,0:T(2,128)(2,1)} %reshape.242), calls=%async_computation.5 | async-start | bytes 1048576 | tf_op jit(solution)/shard_map/all_to_all | solution.py:228
Sparse Core Ops, SparseCore 0:
  116.7 48.6 all-gather.1
  173.6 56.6 reduce-scatter.1
where the time goes:
time: 270 us; the launch traced here: 269 us
  waiting for transfers between devices  145 us (54%)
  blocking collectives  49.4 us (18%)
  starting transfers between devices  32.3 us (12%)
  between operations  13.8 us (5%)
  matrix products  12.5 us (5%)
  local copies, waits for them, and re-layouts  9.64 us (4%)
  other arithmetic  6.72 us (2%)
    reduce_scatter x1, waiting for transfers between devices, shards(): lax.psum_scatter(partial_down.astype(jnp.bfloat16), 'dev_1', scatter_dime...  56.8 us
    all_gather x1, waiting for transfers between devices, shards(): lax.all_gather(arrived.reshape(-1, model_dim), 'dev_1', axis=0, tiled=True)  48.8 us
    all_gather x1, blocking collectives, side_by_side(): lax.all_gather(both, axis, axis=dim, tiled=True)  25.4 us
    all_to_all x1, blocking collectives, shards(): lax.all_to_all(outgoing.reshape(experts * x_count, slot_cap, model_dim),...  24 us
    all_to_all x1, waiting for transfers between devices, shards(): lax.all_to_all(summed.reshape(experts * x_count, slot_cap, model_dim), ('...  16.8 us
    all_to_all x1, waiting for transfers between devices, shards(): lax.all_to_all(payload.reshape(x_count, y_count, block_rows, payload.shap...  12.6 us
    all_to_all x1, starting transfers between devices, shards(): lax.all_to_all(summed.reshape(experts * x_count, slot_cap, model_dim), ('...  11 us
    all_to_all x1, starting transfers between devices, shards(): lax.all_to_all(out_proj.reshape(dev_count, -1, out_proj.shape[1]), DEV, 0...  10.5 us
  transfers between devices with their start and end apart: 6, of which 5 were waited for; matrix products, arithmetic and copies ran while one was open for 3% of the time, Pallas kernels for 0%

commit v1 on v0

--- a/solution.py
+++ b/solution.py
@@ -216,7 +216,12 @@
     arrived = lax.all_to_all(
         outgoing.reshape(experts * x_count, slot_cap, model_dim), ("grp", "dev_0"), 0, 0, tiled=True
     )
-    all_rows = lax.all_gather(arrived.reshape(-1, model_dim), "dev_1", axis=0, tiled=True)
+    all_rows = jnp.concatenate(
+        lax.all_to_all(
+            jnp.stack([arrived.reshape(-1, model_dim)] * lax.axis_size("dev_1")), "dev_1", 0, 0
+        ),
+        axis=0,
+    )
     hid_units = gate_weight.shape[2]
     both_act = jnp.dot(all_rows, both_weight, preferred_element_type=jnp.float32)
     hidden = (jax.nn.silu(both_act[:, :hid_units]) * both_act[:, hid_units:]).astype(jnp.bfloat16)

time: 270 us -> 309 us (1.14)
  blocking collectives: 49.4 us -> 145 us
  waiting for transfers between devices: 145 us -> 91.6 us
    all_to_all x0 -> x1, blocking collectives: none -> 96 us  [shards(): lax.all_to_all(jnp.stack([arrived.reshape(-1, model_dim)] * lax.axis_size...]
    all_gather x1 -> x0, waiting for transfers between devices: 48.8 us -> none  [shards(): lax.all_gather(arrived.reshape(-1, model_dim), 'dev_1', axis=0, tiled=True)]
    reduce_scatter x1, waiting for transfers between devices: 56.8 us -> 52.4 us  [shards(): lax.psum_scatter(partial_down.astype(jnp.bfloat16), 'dev_1', scatter_dime...]
  transfers between devices with their start and end apart: 6 -> 5, of which waited for: 5 -> 4; matrix products, arithmetic and copies ran while one was open for 3% -> 3% of each run, Pallas kernels for 0% -> 0%
where the time goes in v1:
time: 309 us; the launch traced here: 308 us
  blocking collectives  145 us (47%)
  waiting for transfers between devices  91.6 us (30%)
  starting transfers between devices  32.3 us (10%)
  between operations  13.8 us (4%)
  matrix products  10.3 us (3%)
  local copies, waits for them, and re-layouts  8.33 us (3%)
  other arithmetic  6.78 us (2%)
    all_to_all x1, blocking collectives, shards(): lax.all_to_all(jnp.stack([arrived.reshape(-1, model_dim)] * lax.axis_size...  96 us
    reduce_scatter x1, waiting for transfers between devices, shards(): lax.psum_scatter(partial_down.astype(jnp.bfloat16), 'dev_1', scatter_dime...  52.4 us
    all_gather x1, blocking collectives, side_by_side(): lax.all_gather(both, axis, axis=dim, tiled=True)  25.4 us
    all_to_all x1, blocking collectives, shards(): lax.all_to_all(outgoing.reshape(experts * x_count, slot_cap, model_dim),...  23.7 us
    all_to_all x1, waiting for transfers between devices, shards(): lax.all_to_all(summed.reshape(experts * x_count, slot_cap, model_dim), ('...  16.8 us
    all_to_all x1, waiting for transfers between devices, shards(): lax.all_to_all(payload.reshape(x_count, y_count, block_rows, payload.shap...  12.6 us
    all_to_all x1, starting transfers between devices, shards(): lax.all_to_all(summed.reshape(experts * x_count, slot_cap, model_dim), ('...  11 us
    all_to_all x1, starting transfers between devices, shards(): lax.all_to_all(out_proj.reshape(dev_count, -1, out_proj.shape[1]), DEV, 0...  10.5 us
  transfers between devices with their start and end apart: 5, of which 4 were waited for; matrix products, arithmetic and copies ran while one was open for 3% of the time, Pallas kernels for 0%

profile of v1, /device:TPU:1, one launch (start us, length us, event | category | flops | bytes accessed | tf_op | source)
XLA Modules:
  0.0 308.2 jit_solution(9852712527240722028)
XLA Ops:
  6.5 2.1 copy_bitcast_fusion
  8.6 10.5 %all-to-all-start = ((bf16[32,128,64]{1,2,0:T(8,128)(2,1)}), bf16[32,128,64]{1,2,0:T(8,128)(2,1)S(1)}, u32[]{:S(2)}, u32[]{:S(2)}) async-start(bf16[32,128,64]{1,2,0:T(8,128)(2,1)} %copy_bitcast_fusion), calls=%async_computation | async-start | bytes 1048576 | tf_op jit(solution)/shard_map/all_to_all | solution.py:163
  19.3 0.6 reduce-window.6
  21.1 25.4 %all_gather.3 = bf16[16,2,8193]{2,1,0:T(2,128)(2,1)S(1)} all-gather(bf16[1,2,8193]{2,1,0:T(2,128)(2,1)S(1)} %pad_maximum_fusion.1), channel_id=1, replica_groups=mesh['grp'=16,'dev_0'=4,'dev_1'=8] {'grp'}, dimensions={0}, use_global_device_ids=true | all-gather | bytes 557124 | tf_op jit(solution)/shard_map/all_gather | solution.py:16
  46.5 0.7 slice.56
  47.7 0.4 reshape.237
  48.1 0.6 fusion.13
  48.7 0.2 fusion.4
  49.2 0.6 fusion.3
  50.0 0.3 concatenate.28
  50.3 1.5 convolution_convert_fusion
  51.9 4.4 %all-to-all-start.1 = ((bf16[4,8,8,2176]{3,2,1,0:T(8,128)(2,1)}), bf16[4,8,8,2176]{3,2,1,0:T(8,128)(2,1)S(1)}, u32[]{:S(2)}, u32[]{:S(2)}) async-start(bf16[4,8,8,2176]{3,2,1,0:T(8,128)(2,1)} %bitcast.16), calls=%async_computation.1 | async-start | bytes 2228224 | tf_op jit(solution)/shard_map/all_to_all | solution.py:187
  56.5 2.7 pad_maximum_fusion
  59.2 12.6 %all-to-all-done.1 = bf16[4,8,8,2176]{3,2,1,0:T(8,128)(2,1)S(1)} async-done(((bf16[4,8,8,2176]{3,2,1,0:T(8,128)(2,1)}), bf16[4,8,8,2176]{3,2,1,0:T(8,128)(2,1)S(1)}, u32[]{:S(2)}, u32[]{:S(2)}) %all-to-all-start.1) | async-done | bytes 1114144 | tf_op jit(solution)/shard_map/all_to_all | solution.py:187
  71.8 1.0 reduce_sum.87
  72.7 6.4 %all-to-all-start.2 = ((bf16[8,8,2176]{2,1,0:T(8,128)(2,1)}), bf16[8,8,2176]{2,1,0:T(8,128)(2,1)S(1)}, u32[]{:S(2)}, u32[]{:S(2)}) async-start(bf16[8,8,2176]{2,1,0:T(8,128)(2,1)} %reduce_sum.87), calls=%async_computation.2 | async-start | bytes 557056 | tf_op jit(solution)/shard_map/all_to_all | solution.py:193
  79.7 9.8 %all-to-all-done.2 = bf16[8,8,2176]{2,1,0:T(8,128)(2,1)S(1)} async-done(((bf16[8,8,2176]{2,1,0:T(8,128)(2,1)}), bf16[8,8,2176]{2,1,0:T(8,128)(2,1)S(1)}, u32[]{:S(2)}, u32[]{:S(2)}) %all-to-all-start.2) | async-done | bytes 278560 | tf_op jit(solution)/shard_map/all_to_all | solution.py:193
  89.9 0.2 convolution_convert_fusion.2
  90.3 0.3 broadcast_in_dim.79
  90.6 23.7 %all_to_all.30 = bf16[64,2,2048]{2,1,0:T(2,128)(2,1)S(1)} all-to-all(bf16[64,2,2048]{2,1,0:T(2,128)(2,1)S(1)} %bitcast.84), channel_id=1, replica_groups=mesh['grp'=16,'dev_0'=4,'dev_1'=8] {'grp','dev_0'}, dimensions={0} | all-to-all | bytes 1048576 | tf_op jit(solution)/shard_map/all_to_all | solution.py:216
  114.5 0.5 stack.3
  115.1 96.0 %all_to_all.31 = bf16[8,128,2048]{2,1,0:T(8,128)(2,1)S(1)} all-to-all(bf16[8,128,2048]{2,1,0:T(8,128)(2,1)S(1)} %stack.3), channel_id=1, replica_groups=mesh['grp'=16,'dev_0'=4,'dev_1'=8] {'dev_1'}, dimensions={0} | all-to-all | bytes 8388608 | tf_op jit(solution)/shard_map/all_to_all | solution.py:220
  211.1 2.3 fusion.63
  213.4 0.3 fusion.10
  213.8 3.2 %convolution_convert_fusion.1 = bf16[1024,2048]{1,0:T(8,128)(2,1)} fusion(bf16[1024,256]{1,0:T(8,128)(2,1)S(1)} %fusion.10, bf16[1,256,2048]{2,1,0:T(8,128)(2,1)S(1)} %copy-done), kind=kOutput, calls=%fused_computation.1 | convolution fusion | flops 1075838976 | bytes 5767168 | tf_op jit(solution)/shard_map/dot_general | solution.py:229
  217.0 52.4 %reduce-scatter.2.cloned.1.call-done = bf16[128,2048]{1,0:T(8,128)(2,1)} async-done(((bf16[1024,2048]{1,0:T(8,128)(2,1)}), bf16[128,2048]{1,0:T(8,128)(2,1)}) %reduce-scatter.2.cloned.1.call-update) | async-done | bytes 524304 | tf_op jit(solution)/shard_map/reduce_scatter | solution.py:230
  269.4 2.2 reshape.244
  271.6 11.0 %all-to-all-start.5 = ((bf16[64,2,2048]{2,1,0:T(2,128)(2,1)}), bf16[64,2,2048]{2,1,0:T(2,128)(2,1)S(1)}, u32[]{:S(2)}, u32[]{:S(2)}) async-start(bf16[64,2,2048]{2,1,0:T(2,128)(2,1)} %reshape.244), calls=%async_computation.6 | async-start | bytes 1048576 | tf_op jit(solution)/shard_map/all_to_all | solution.py:233
  282.6 0.3 select_reduce_fusion.2
  283.0 16.8 %all-to-all-done.5 = bf16[64,2,2048]{2,1,0:T(2,128)(2,1)S(1)} async-done(((bf16[64,2,2048]{2,1,0:T(2,128)(2,1)}), bf16[64,2,2048]{2,1,0:T(2,128)(2,1)S(1)}, u32[]{:S(2)}, u32[]{:S(2)}) %all-to-all-start.5) | async-done | bytes 524320 | tf_op jit(solution)/shard_map/all_to_all | solution.py:233
  299.8 0.5 convert_reduce_fusion
  300.5 0.9 fusion.1
  (80 shorter events, 3.9 us)
Async XLA Ops:
  6.5 207.2 %copy-start = (bf16[1,256,2048]{2,1,0:T(8,128)(2,1)S(1)}, bf16[1,256,2048]{2,1,0:T(8,128)(2,1)}, u32[]{:S(2)}) copy-start(bf16[1,256,2048]{2,1,0:T(8,128)(2,1)} %param.31) | copy-start | bytes 3145732
  6.5 12.6 %copy-start.9 = (f32[256,2]{0,1:T(2,128)S(1)}, f32[256,2]{0,1:T(2,128)}, u32[]{:S(2)}) copy-start(f32[256,2]{0,1:T(2,128)} %param.18) | copy-start | bytes 6148
  6.5 12.6 %copy-start.12 = (f32[2]{0:T(128)S(1)}, f32[2]{0:T(128)}, u32[]{:S(2)}) copy-start(f32[2]{0:T(128)} %param.19) | copy-start | bytes 28
  6.5 14.0 %copy-start.6 = (bf16[256,128]{1,0:T(8,128)(2,1)S(1)}, bf16[256,128]{1,0:T(8,128)(2,1)}, u32[]{:S(2)}) copy-start(bf16[256,128]{1,0:T(8,128)(2,1)} %param.16) | copy-start | bytes 196612
  6.5 14.2 %copy-start.3 = (bf16[256,128]{1,0:T(8,128)(2,1)S(1)}, bf16[256,128]{1,0:T(8,128)(2,1)}, u32[]{:S(2)}) copy-start(bf16[256,128]{1,0:T(8,128)(2,1)} %param.20) | copy-start | bytes 196612
  8.6 41.4 %all-to-all-start = ((bf16[32,128,64]{1,2,0:T(8,128)(2,1)}), bf16[32,128,64]{1,2,0:T(8,128)(2,1)S(1)}, u32[]{:S(2)}, u32[]{:S(2)}) async-start(bf16[32,128,64]{1,2,0:T(8,128)(2,1)} %copy_bitcast_fusion), calls=%async_computation | async-start | bytes 1048576 | tf_op jit(solution)/shard_map/all_to_all | solution.py:163
  19.1 29.5 %copy-start.4 = (bf16[256,128]{1,0:T(8,128)(2,1)S(1)}, bf16[256,128]{1,0:T(8,128)(2,1)}, u32[]{:S(2)}) copy-start(bf16[256,128]{1,0:T(8,128)(2,1)} %param.21) | copy-start | bytes 196612
  20.9 28.2 %copy-start.14 = (f32[2]{0:T(128)S(1)}, f32[2]{0:T(128)}, u32[]{:S(2)}) copy-start(f32[2]{0:T(128)} %param.22) | copy-start | bytes 28
  47.2 2.7 copy-start.5
  47.2 2.7 copy-start.11
  51.9 4.4 %copy-start.10 = (s32[8,2]{0,1:T(2,128)S(1)}, s32[8,2]{0,1:T(2,128)}, u32[]{:S(2)}) copy-start(s32[8,2]{0,1:T(2,128)} %param.28) | copy-start | bytes 196
  51.9 4.6 %copy-start.2 = (bf16[1,2048,256]{2,1,0:T(8,128)(2,1)S(1)}, bf16[1,2048,256]{2,1,0:T(8,128)(2,1)}, u32[]{:S(2)}) copy-start(bf16[1,2048,256]{2,1,0:T(8,128)(2,1)} %param.30) | copy-start | bytes 3145732
  51.9 19.9 %all-to-all-start.1 = ((bf16[4,8,8,2176]{3,2,1,0:T(8,128)(2,1)}), bf16[4,8,8,2176]{3,2,1,0:T(8,128)(2,1)S(1)}, u32[]{:S(2)}, u32[]{:S(2)}) async-start(bf16[4,8,8,2176]{3,2,1,0:T(8,128)(2,1)} %bitcast.16), calls=%async_computation.1 | async-start | bytes 2228224 | tf_op jit(solution)/shard_map/all_to_all | solution.py:187
  59.2 30.4 %copy-start.7 = (bf16[8,2048]{1,0:T(8,128)(2,1)S(1)}, bf16[8,2048]{1,0:T(8,128)(2,1)}, u32[]{:S(2)}) copy-start(bf16[8,2048]{1,0:T(8,128)(2,1)} %param.25) | copy-start | bytes 98308
  59.2 30.7 %copy-start.8 = (f32[2048]{0:T(1024)S(1)}, f32[2048]{0:T(1024)}, u32[]{:S(2)}) copy-start(f32[2048]{0:T(1024)} %param.26) | copy-start | bytes 24580
  72.7 16.8 %all-to-all-start.2 = ((bf16[8,8,2176]{2,1,0:T(8,128)(2,1)}), bf16[8,8,2176]{2,1,0:T(8,128)(2,1)S(1)}, u32[]{:S(2)}, u32[]{:S(2)}) async-start(bf16[8,8,2176]{2,1,0:T(8,128)(2,1)} %reduce_sum.87), calls=%async_computation.2 | async-start | bytes 557056 | tf_op jit(solution)/shard_map/all_to_all | solution.py:193
  79.1 190.3 %reduce-scatter.2.cloned.1.call-start = ((), (), s32[]{:S(2)}) async-start(), calls=%async_computation.7 | async-start | bytes 4718592 | tf_op jit(solution)/shard_map/reduce_scatter | solution.py:230
  115.1 96.0 %copy-start.1 = (bf16[2048,512]{1,0:T(8,128)(2,1)S(1)}, bf16[2048,512]{1,0:T(8,128)(2,1)}, u32[]{:S(2)}) copy-start(bf16[2048,512]{1,0:T(8,128)(2,1)} %pad_maximum_fusion) | copy-start | bytes 6291460
  217.0 65.7 %copy-start.13 = (f32[2048,16]{0,1:T(8,128)S(1)}, f32[2048,16]{0,1:T(8,128)}, u32[]{:S(2)}) copy-start(f32[2048,16]{0,1:T(8,128)} %param.27) | copy-start | bytes 393220
  271.6 28.2 %all-to-all-start.5 = ((bf16[64,2,2048]{2,1,0:T(2,128)(2,1)}), bf16[64,2,2048]{2,1,0:T(2,128)(2,1)S(1)}, u32[]{:S(2)}, u32[]{:S(2)}) async-start(bf16[64,2,2048]{2,1,0:T(2,128)(2,1)} %reshape.244), calls=%async_computation.6 | async-start | bytes 1048576 | tf_op jit(solution)/shard_map/all_to_all | solution.py:233
Sparse Core Ops, SparseCore 0:
  217.1 52.2 reduce-scatter.1
